TPU v7x, 32 devices: a whole 2x2x4 slice. The times are simulated.
32 devices in a mesh: seq: 2 (over x), ctx: 8 (over z, y), wsh: 2 (over core).
Axes of the slice: x: 2, y: 2, z: 4, core: 2. Of those that a mesh axis runs over, the one named last changes fastest.
Arguments:
- layer_in: bfloat16 [2, 1024, 896], P('seq', 'ctx'), may hold values from -6 to 6
- grad_out: bfloat16 [2, 1024, 896], P('seq', 'ctx'), may hold values from -6 to 6
- positions: int32 [2, 1024], P('seq'), may hold values from 0 to 1023, as said below
- attn_gain: bfloat16 [896], P(('seq', 'ctx', 'wsh')), may hold values from 0.099609375 to 1.8984375
- w_query: bfloat16 [896, 896], P(('seq', 'ctx'), 'wsh'), may hold values from -0.1875 to 0.1875
- b_query: bfloat16 [896], P(('seq', 'ctx', 'wsh')), may hold values from -3 to 3
- w_keyvalue: bfloat16 [896, 256], P(('seq', 'ctx'), 'wsh'), may hold values from -0.1875 to 0.1875
- b_keyvalue: bfloat16 [256], P(('seq', 'ctx', 'wsh')), may hold values from -3 to 3
- w_output: bfloat16 [896, 896], P('wsh', ('seq', 'ctx')), may hold values from -3 to 3
- mlp_gain: bfloat16 [896], P(('seq', 'ctx', 'wsh')), may hold values from 0.099609375 to 1.8984375
- w_gate: bfloat16 [896, 4864], P(('seq', 'ctx'), 'wsh'), may hold values from -0.1875 to 0.1875
- w_up: bfloat16 [896, 4864], P(('seq', 'ctx'), 'wsh'), may hold values from -0.1875 to 0.1875
- w_down: bfloat16 [4864, 896], P('wsh', ('seq', 'ctx')), may hold values from -0.078125 to 0.078125
Outputs:
- layer_out: bfloat16 [2, 1024, 896], P('seq', 'ctx')
- grad_in: bfloat16 [2, 1024, 896], P('seq', 'ctx')
- grad_attn_gain: float32 [896], P(('seq', 'ctx', 'wsh'))
- grad_w_query: float32 [896, 896], P(('seq', 'ctx'), 'wsh')
- grad_b_query: float32 [896], P(('seq', 'ctx', 'wsh'))
- grad_w_keyvalue: float32 [896, 256], P(('seq', 'ctx'), 'wsh')
- grad_b_keyvalue: float32 [256], P(('seq', 'ctx', 'wsh'))
- grad_w_output: float32 [896, 896], P('wsh', ('seq', 'ctx'))
- grad_mlp_gain: float32 [896], P(('seq', 'ctx', 'wsh'))
- grad_w_gate: float32 [896, 4864], P(('seq', 'ctx'), 'wsh')
- grad_w_up: float32 [896, 4864], P(('seq', 'ctx'), 'wsh')
- grad_w_down: float32 [4864, 896], P('wsh', ('seq', 'ctx'))
Inputs may be any that keep to these rules, and one draw needn't show every extreme that they name: Each row (one sequence) holds every position 0 to 1023 once; the 128 rows of one index of ctx are two blocks of 64 consecutive positions, block p then block 15 - p, with the pair p of each index drawn per sequence.
All inputs are finite; a program needn't handle non-finite values.
Results may differ from a plain program's by a relative error of at most 0.018.
Values may be sent and summed in bfloat16 or wider, within the bound.
No kernel may reach another device: no remote copies, remote signals or barrier semaphores. Data moves between devices by JAX's collectives and lax.ppermute only.
A program may use at most 192 MiB of HBM per device.

v0:
```python
import math
import jax
import jax.numpy as jnp
from jax import lax
from jax.sharding import PartitionSpec as P

HD = 64
epsilon = 1e-06
theta_log = math.log(1000000.0)


def partner(block, axis, stride):
    count = lax.axis_size(axis)
    route = []
    for low in range(count):
        high = low | 1 << stride
        if high != low and high < count:
            route += [(low, high), (high, low)]
    return lax.ppermute(block, axis, route)


def rope_tables(positions, half_dim):
    inv_freq = jnp.exp(-jnp.arange(half_dim, dtype=jnp.float32) * (theta_log / half_dim))
    turned = positions.astype(jnp.float32)[:, None] * inv_freq[None, :]
    return (jnp.cos(turned)[:, None, :], jnp.sin(turned)[:, None, :])


def rotate(values, cos_tab, sin_tab):
    half_dim = values.shape[-1] // 2
    first_half = values[..., :half_dim]
    second_half = values[..., half_dim:]
    return jnp.concatenate(
        [
            first_half * cos_tab - second_half * sin_tab,
            second_half * cos_tab + first_half * sin_tab,
        ],
        axis=-1,
    )


def left_inner(left_mat, right_mat):
    return lax.dot_general(
        left_mat, right_mat, (((0,), (0,)), ((), ())), preferred_element_type=jnp.float32
    )


def right_inner(left_mat, right_mat):
    return lax.dot_general(
        left_mat, right_mat, (((1,), (1,)), ((), ())), preferred_element_type=jnp.float32
    )


def norm_back(grad_normed, normed_hat, scale_inv, gain_vec):
    weighted = grad_normed * gain_vec
    return scale_inv * (
        weighted - normed_hat * jnp.mean(weighted * normed_hat, axis=-1, keepdims=True)
    )


def halve_sum(buffer, sender, group_count, group_index):
    for bit_pos in reversed(range(group_count.bit_length() - 1)):
        half_rows = buffer.shape[0] // 2
        my_bit = group_index >> bit_pos & 1
        kept_rows = lax.dynamic_slice_in_dim(buffer, my_bit * half_rows, half_rows, 0)
        outgoing = lax.dynamic_slice_in_dim(buffer, (1 - my_bit) * half_rows, half_rows, 0)
        buffer = kept_rows + sender(outgoing, bit_pos)
    return buffer


def per_device(
    layer_in,
    grad_out,
    positions,
    attn_gain,
    w_query,
    b_query,
    w_keyvalue,
    b_keyvalue,
    w_output,
    mlp_gain,
    w_gate,
    w_up,
    w_down,
):
    wq_full, wkv_full, wo_full, wg_full, wu_full, wd_full = (
        lax.all_gather(w_query, ("seq", "ctx"), axis=0, tiled=True),
        lax.all_gather(w_keyvalue, ("seq", "ctx"), axis=0, tiled=True),
        lax.all_gather(w_output, ("seq", "ctx"), axis=1, tiled=True),
        lax.all_gather(w_gate, ("seq", "ctx"), axis=0, tiled=True),
        lax.all_gather(w_up, ("seq", "ctx"), axis=0, tiled=True),
        lax.all_gather(w_down, ("seq", "ctx"), axis=1, tiled=True),
    )
    g_one, bias_q, bias_kv, g_two = (
        lax.all_gather(attn_gain, ("seq", "ctx", "wsh"), axis=0, tiled=True),
        lax.all_gather(b_query, ("seq", "ctx", "wsh"), axis=0, tiled=True),
        lax.all_gather(b_keyvalue, ("seq", "ctx", "wsh"), axis=0, tiled=True),
        lax.all_gather(mlp_gain, ("seq", "ctx", "wsh"), axis=0, tiled=True),
    )
    shard_id = lax.axis_index("wsh")
    group_count = lax.axis_size(("seq", "ctx"))
    group_index = lax.axis_index(("seq", "ctx"))
    q_cols = wq_full.shape[1]
    kv_cols = wkv_full.shape[1]
    ff_cols = wg_full.shape[1]
    bias_q = lax.dynamic_slice_in_dim(bias_q, shard_id * q_cols, q_cols).astype(jnp.float32)
    bias_kv = lax.dynamic_slice_in_dim(bias_kv, shard_id * kv_cols, kv_cols).astype(jnp.float32)
    g_one = g_one.astype(jnp.float32)
    g_two = g_two.astype(jnp.float32)
    row_count = layer_in.shape[1]
    head_count = q_cols // HD
    seq_len = positions.shape[1]
    score_scale = 1.0 / math.sqrt(HD)
    pos_all = positions[0]
    pos_mine = lax.dynamic_slice_in_dim(pos_all, lax.axis_index("ctx") * row_count, row_count)
    x_full = layer_in[0].astype(jnp.float32)
    scale_one = lax.rsqrt(jnp.mean(x_full * x_full, axis=-1, keepdims=True) + epsilon)
    hat_one = x_full * scale_one
    normed_one = (hat_one * g_one).astype(jnp.bfloat16)
    query_pre = jnp.dot(normed_one, wq_full, preferred_element_type=jnp.float32) + bias_q
    kv_pre = jnp.dot(normed_one, wkv_full, preferred_element_type=jnp.float32) + bias_kv
    cos_tab, sin_tab = rope_tables(pos_mine, HD // 2)
    query_low = rotate(query_pre.reshape(row_count, head_count, HD), cos_tab, sin_tab).astype(
        jnp.bfloat16
    )
    key_low = rotate(kv_pre[:, None, :HD], cos_tab, sin_tab)[:, 0, :].astype(jnp.bfloat16)
    value_low = kv_pre[:, HD:].astype(jnp.bfloat16)
    kv_all = lax.all_gather(
        jnp.concatenate([key_low, value_low], axis=1), "ctx", axis=0, tiled=True
    )
    k_rows = math.gcd(seq_len, 512)
    blocks_n = seq_len // k_rows
    kv_blocks = kv_all.reshape(blocks_n, k_rows, 2 * HD)
    pos_blocks = pos_all.reshape(blocks_n, k_rows)

    def block_scores(kv_block, pos_block):
        scores = (
            jnp.einsum(
                "qhd,kd->hqk", query_low, kv_block[:, :HD], preferred_element_type=jnp.float32
            )
            * score_scale
        )
        allowed = pos_block[None, :] <= pos_mine[:, None]
        return jnp.where(allowed[None], scores, -1e30)

    def stats_step(run_state, kv_pair):
        run_max, run_sum = run_state
        scores = block_scores(kv_pair[0], kv_pair[1])
        new_max = jnp.maximum(run_max, jnp.max(scores, axis=-1))
        run_sum = run_sum * jnp.exp(run_max - new_max) + jnp.sum(
            jnp.exp(scores - new_max[..., None]), axis=-1
        )
        return ((new_max, run_sum), None)

    init_max = jnp.full((head_count, row_count), -1e30, jnp.float32)
    init_sum = jnp.zeros((head_count, row_count), jnp.float32)
    (run_max, run_sum), unused = lax.scan(stats_step, (init_max, init_sum), (kv_blocks, pos_blocks))
    log_sum = run_max + jnp.log(run_sum)

    def out_step(run_state, kv_pair):
        sum_low, sum_full = run_state
        scores = block_scores(kv_pair[0], kv_pair[1])
        prob_full = jnp.exp(scores - log_sum[..., None])
        prob_low = prob_full.astype(jnp.bfloat16)
        value_blk = kv_pair[0][:, HD:]
        sum_low = sum_low + jnp.einsum(
            "hqk,kd->hqd", prob_low, value_blk, preferred_element_type=jnp.float32
        )
        sum_full = sum_full + jnp.einsum(
            "hqk,kd->hqd",
            prob_full,
            value_blk.astype(jnp.float32),
            preferred_element_type=jnp.float32,
        )
        return ((sum_low, sum_full), None)

    zero_heads = jnp.zeros((head_count, row_count, HD), jnp.float32)
    (attended, attended_exact), unused = lax.scan(
        out_step, (zero_heads, zero_heads), (kv_blocks, pos_blocks)
    )
    attended_low = (
        jnp.transpose(attended, (1, 0, 2)).reshape(row_count, head_count * HD).astype(jnp.bfloat16)
    )
    branch = lax.psum(jnp.dot(attended_low, wo_full, preferred_element_type=jnp.float32), "wsh")
    hidden = x_full + branch
    scale_two = lax.rsqrt(jnp.mean(hidden * hidden, axis=-1, keepdims=True) + epsilon)
    hat_two = hidden * scale_two
    normed_two = (hat_two * g_two).astype(jnp.bfloat16)
    gate_pre = jnp.dot(normed_two, wg_full, preferred_element_type=jnp.float32)
    up_proj = jnp.dot(normed_two, wu_full, preferred_element_type=jnp.float32)
    act_low = (jax.nn.silu(gate_pre) * up_proj).astype(jnp.bfloat16)
    mlp_out = lax.psum(
        jnp.dot(act_low, wd_full, preferred_element_type=jnp.float32).astype(jnp.bfloat16), "wsh"
    ).astype(jnp.float32)
    layer_out = (hidden + mlp_out).astype(jnp.bfloat16)
    wq_full, wkv_full, wo_full, wg_full, wu_full, wd_full = (
        lax.all_gather(w_query, ("seq", "ctx"), axis=0, tiled=True),
        lax.all_gather(w_keyvalue, ("seq", "ctx"), axis=0, tiled=True),
        lax.all_gather(w_output, ("seq", "ctx"), axis=1, tiled=True),
        lax.all_gather(w_gate, ("seq", "ctx"), axis=0, tiled=True),
        lax.all_gather(w_up, ("seq", "ctx"), axis=0, tiled=True),
        lax.all_gather(w_down, ("seq", "ctx"), axis=1, tiled=True),
    )
    grad_low = grad_out[0]
    grad_full = grad_low.astype(jnp.float32)
    grad_act = right_inner(grad_low, wd_full)
    gw_down_t = left_inner(grad_low, act_low)
    sigmoid_g = jax.nn.sigmoid(gate_pre)
    grad_up = (grad_act * (gate_pre * sigmoid_g)).astype(jnp.bfloat16)
    grad_gate = (grad_act * up_proj * sigmoid_g * (1.0 + gate_pre * (1.0 - sigmoid_g))).astype(
        jnp.bfloat16
    )
    gw_gate = left_inner(normed_two, grad_gate)
    gw_up = left_inner(normed_two, grad_up)
    part_two = right_inner(grad_gate, wg_full) + right_inner(grad_up, wu_full)
    gg_two = jnp.sum(part_two * hat_two, axis=0)
    grad_normed_two = lax.psum(part_two.astype(jnp.bfloat16), "wsh").astype(jnp.float32)
    grad_hidden = grad_full + norm_back(grad_normed_two, hat_two, scale_two, g_two)
    hidden_low = grad_hidden.astype(jnp.bfloat16)
    gw_out_t = left_inner(hidden_low, attended_low)
    grad_att = (
        right_inner(hidden_low, wo_full).reshape(row_count, head_count, HD).astype(jnp.bfloat16)
    )
    row_delta = jnp.sum(
        jnp.transpose(grad_att.astype(jnp.float32), (1, 0, 2)) * attended_exact, axis=-1
    )

    def back_step(grad_q, kv_pair):
        kv_block, pos_block = kv_pair
        scores = block_scores(kv_block, pos_block)
        prob_full = jnp.exp(scores - log_sum[..., None])
        prob_low = prob_full.astype(jnp.bfloat16)
        grad_prob = jnp.einsum(
            "qhd,kd->hqk", grad_att, kv_block[:, HD:], preferred_element_type=jnp.float32
        )
        grad_score = (prob_full * (grad_prob - row_delta[..., None])).astype(jnp.bfloat16)
        grad_q = grad_q + jnp.einsum(
            "hqk,kd->qhd", grad_score, kv_block[:, :HD], preferred_element_type=jnp.float32
        )
        grad_key = jnp.einsum(
            "hqk,qhd->kd", grad_score, query_low, preferred_element_type=jnp.float32
        )
        grad_value = jnp.einsum(
            "hqk,qhd->kd", prob_low, grad_att, preferred_element_type=jnp.float32
        )
        return (grad_q, jnp.concatenate([grad_key * score_scale, grad_value], axis=1))

    grad_q, kv_terms = lax.scan(
        back_step, jnp.zeros((row_count, head_count, HD), jnp.float32), (kv_blocks, pos_blocks)
    )
    grad_q = grad_q * score_scale
    grad_kv = lax.psum_scatter(
        kv_terms.reshape(seq_len, 2 * HD).astype(jnp.bfloat16),
        "ctx",
        scatter_dimension=0,
        tiled=True,
    ).astype(jnp.float32)
    grad_qpre = (
        rotate(grad_q, cos_tab, -sin_tab).reshape(row_count, head_count * HD).astype(jnp.bfloat16)
    )
    grad_kpre = rotate(grad_kv[:, None, :HD], cos_tab, -sin_tab)[:, 0, :]
    grad_kvpre = jnp.concatenate([grad_kpre, grad_kv[:, HD:]], axis=1).astype(jnp.bfloat16)
    gw_query = left_inner(normed_one, grad_qpre)
    gw_kv = left_inner(normed_one, grad_kvpre)
    wsh_count = lax.axis_size("wsh")
    gb_q_full = lax.dynamic_update_slice_in_dim(
        jnp.zeros((q_cols * wsh_count,), jnp.float32),
        jnp.sum(grad_qpre.astype(jnp.float32), axis=0),
        shard_id * q_cols,
        0,
    )
    gb_kv_full = lax.dynamic_update_slice_in_dim(
        jnp.zeros((kv_cols * wsh_count,), jnp.float32),
        jnp.sum(grad_kvpre.astype(jnp.float32), axis=0),
        shard_id * kv_cols,
        0,
    )
    part_one = right_inner(grad_qpre, wq_full) + right_inner(grad_kvpre, wkv_full)
    gg_one = jnp.sum(part_one * hat_one, axis=0)
    grad_normed_one = lax.psum(part_one.astype(jnp.bfloat16), "wsh").astype(jnp.float32)
    grad_input = (grad_hidden + norm_back(grad_normed_one, hat_one, scale_one, g_one)).astype(
        jnp.bfloat16
    )
    out_g_one, out_b_q, out_b_kv, out_g_two = (
        lax.psum_scatter(gg_one, ("seq", "ctx", "wsh"), scatter_dimension=0, tiled=True),
        lax.psum_scatter(gb_q_full, ("seq", "ctx", "wsh"), scatter_dimension=0, tiled=True),
        lax.psum_scatter(gb_kv_full, ("seq", "ctx", "wsh"), scatter_dimension=0, tiled=True),
        lax.psum_scatter(gg_two, ("seq", "ctx", "wsh"), scatter_dimension=0, tiled=True),
    )
    all_owned = lax.psum_scatter(
        jnp.concatenate([gw_query, gw_kv, gw_out_t, gw_gate, gw_up, gw_down_t], axis=1).astype(
            jnp.bfloat16
        ),
        ("seq", "ctx"),
        scatter_dimension=0,
        tiled=True,
    ).astype(jnp.float32)
    proj_owned = all_owned[:, : 2 * q_cols + kv_cols]
    mlp_owned = all_owned[:, 2 * q_cols + kv_cols :]
    out_wq = proj_owned[:, :q_cols]
    out_wkv = proj_owned[:, q_cols : q_cols + kv_cols]
    out_wo = jnp.transpose(proj_owned[:, q_cols + kv_cols :])
    out_wg = mlp_owned[:, :ff_cols]
    out_wu = mlp_owned[:, ff_cols : 2 * ff_cols]
    out_wd = jnp.transpose(mlp_owned[:, 2 * ff_cols :])
    return (
        layer_out[None],
        grad_input[None],
        out_g_one,
        out_wq,
        out_b_q,
        out_wkv,
        out_b_kv,
        out_wo,
        out_g_two,
        out_wg,
        out_wu,
        out_wd,
    )


def solution(mesh):
    return jax.shard_map(
        per_device,
        mesh=mesh,
        in_specs=(
            P("seq", "ctx", None),
            P("seq", "ctx", None),
            P("seq", None),
            P(("seq", "ctx", "wsh")),
            P(("seq", "ctx"), "wsh"),
            P(("seq", "ctx", "wsh")),
            P(("seq", "ctx"), "wsh"),
            P(("seq", "ctx", "wsh")),
            P("wsh", ("seq", "ctx")),
            P(("seq", "ctx", "wsh")),
            P(("seq", "ctx"), "wsh"),
            P(("seq", "ctx"), "wsh"),
            P("wsh", ("seq", "ctx")),
        ),
        out_specs=(
            P("seq", "ctx", None),
            P("seq", "ctx", None),
            P(("seq", "ctx", "wsh")),
            P(("seq", "ctx"), "wsh"),
            P(("seq", "ctx", "wsh")),
            P(("seq", "ctx"), "wsh"),
            P(("seq", "ctx", "wsh")),
            P("wsh", ("seq", "ctx")),
            P(("seq", "ctx", "wsh")),
            P(("seq", "ctx"), "wsh"),
            P(("seq", "ctx"), "wsh"),
            P("wsh", ("seq", "ctx")),
        ),
        check_vma=False,
    )
```

profile of v0, /device:TPU:0, one launch (start us, length us, event | category | flops | bytes accessed | tf_op | source)
XLA Modules:
  0.0 914.5 jit_solution(13022958622151075140)
XLA Ops:
  12.6 42.1 %all-reduce.10 = (bf16[256]{0:T(256)(128)(2,1)S(1)}, bf16[896]{0:T(1024)(128)(2,1)S(1)}, bf16[896]{0:T(1024)(128)(2,1)S(1)}, bf16[896]{0:T(1024)(128)(2,1)S(1)}) all-reduce(bf16[256]{0:T(256)(128)(2,1)S(1)} %dynamic-update-slice.1, bf16[896]{0:T(1024)(128)(2,1)S(1)} %dynamic-update-slice, ...), channel_id=1, replica_groups=mesh['seq'=2,'ctx'=8,'wsh'=2] {'seq','ctx','wsh'}, use_global_device_ids=true, to_apply=%add.1 | all-reduce | flops 2944 | bytes 11776
  54.7 41.0 %all_gather.40 = bf16[896,128]{1,0:T(8,128)(2,1)S(1)} all-gather(bf16[56,128]{1,0:T(8,128)(2,1)} %param.25), channel_id=1, replica_groups=mesh['seq'=2,'ctx'=8,'wsh'=2] {'seq','ctx'}, dimensions={0}, use_global_device_ids=true | all-gather | bytes 243712 | tf_op jit(solution)/shard_map/all_gather | solution.py:87
  99.9 26.7 %all_gather.42 = bf16[1024,128]{0,1:T(8,128)(2,1)S(1)} all-gather(bf16[128,128]{0,1:T(8,128)(2,1)S(1)} %pad_maximum_fusion.1), channel_id=1, replica_groups=mesh['seq'=2,'ctx'=8,'wsh'=2] {'ctx'}, dimensions={0}, use_global_device_ids=true | all-gather | bytes 294912 | tf_op jit(solution)/shard_map/all_gather | solution.py:127
  126.6 42.1 %all_gather.43 = bf16[896,448]{1,0:T(8,128)(2,1)S(1)} all-gather(bf16[56,448]{1,0:T(8,128)(2,1)S(1)} %copy-done.17), channel_id=1, replica_groups=mesh['seq'=2,'ctx'=8,'wsh'=2] {'seq','ctx'}, dimensions={0}, use_global_device_ids=true | all-gather | bytes 852992 | tf_op jit(solution)/shard_map/all_gather | solution.py:86
  169.4 2.2 while.39
  171.6 2.9 while.40
  174.6 42.6 %all_gather.45 = bf16[448,896]{0,1:T(8,128)(2,1)S(1)} all-gather(bf16[448,56]{0,1:T(8,128)(2,1)S(1)} %copy-done.18), channel_id=1, replica_groups=mesh['seq'=2,'ctx'=8,'wsh'=2] {'seq','ctx'}, dimensions={1}, use_global_device_ids=true | all-gather | bytes 852992 | tf_op jit(solution)/shard_map/all_gather | solution.py:88
  220.3 13.9 %all-reduce.16.cloned.1.call-done = f32[128,896]{1,0:T(8,128)} async-done(((f32[128,896]{1,0:T(8,128)}), f32[128,896]{1,0:T(8,128)}) %all-reduce.16.cloned.1.call-update) | async-done | bytes 458768 | tf_op jit(solution)/shard_map/psum | solution.py:183
  235.5 60.1 %all-gather.6.cloned.1.call-done = bf16[896,2432]{1,0:T(8,128)(2,1)} async-done(((bf16[56,2432]{1,0:T(8,128)(2,1)}), bf16[896,2432]{1,0:T(8,128)(2,1)}) %all-gather.6.cloned.1.call-update) | async-done | bytes 4358160 | tf_op jit(solution)/shard_map/all_gather | solution.py:90
  295.5 4.1 fusion.76
  299.7 73.9 %all-gather.4.cloned.1.call-done = bf16[896,2432]{1,0:T(8,128)(2,1)} async-done(((bf16[56,2432]{1,0:T(8,128)(2,1)}), bf16[896,2432]{1,0:T(8,128)(2,1)}) %all-gather.4.cloned.1.call-update) | async-done | bytes 4358160 | tf_op jit(solution)/shard_map/all_gather | solution.py:89
  373.6 4.1 fusion.75
  377.7 73.9 %all-gather.8.cloned.1.call-done = bf16[2432,896]{0,1:T(8,128)(2,1)} async-done(((bf16[2432,56]{0,1:T(8,128)(2,1)}), bf16[2432,896]{0,1:T(8,128)(2,1)}) %all-gather.8.cloned.1.call-update) | async-done | bytes 4358160 | tf_op jit(solution)/shard_map/all_gather | solution.py:91
  451.6 5.0 multiply_convert_fusion
  456.6 3.4 convolution_convert_fusion.1
  461.3 4.4 fusion.72
  466.0 4.6 fusion.14
  470.6 4.4 convolution_convert_fusion.6
  474.9 3.5 convolution_convert_fusion.2
  478.4 4.2 all-reduce.18.cloned.1.call-done
  482.6 1.3 multiply_reduce_fusion
  487.1 6.6 while.41
  493.6 1.8 copy.59
  495.5 1.5 copy.50
  498.4 60.5 %reduce-scatter.8.cloned.1.call-done = bf16[128,128]{1,0:T(8,128)(2,1)} async-done(((bf16[1024,128]{1,0:T(8,128)(2,1)}), bf16[128,128]{1,0:T(8,128)(2,1)}) %reduce-scatter.8.cloned.1.call-update) | async-done | bytes 32784
  560.2 2.1 fusion.73
  563.8 1.5 copy.48
  565.7 25.7 %concatenate.35 = bf16[896,8320]{1,0:T(8,128)(2,1)} concatenate(bf16[896,448]{1,0:T(8,128)(2,1)S(1)} %copy.48, bf16[896,128]{1,0:T(8,128)(2,1)S(1)} %copy.49, bf16[896,448]{1,0:T(8,128)(2,1)S(1)} %copy.50, bf16[896,2432]{1,0:T(8,128)(2,1)} %convolution_convert_fusion.2, bf16[896,2432]{1,0:T(8,128)(2,1)} %convolution_convert_fusion.1, bf16[896,2432]{1,0:T(8,128)(2,1)} %fusion.14), dimensions={1} | concatenate | bytes 29818880 | tf_op jit(solution)/shard_map/concatenate | solution.py:290
  593.6 68.7 %all-reduce.9 = (f32[896]{0:T(1024)S(1)}, f32[896]{0:T(1024)S(1)}, f32[256]{0:T(256)S(1)}, f32[896]{0:T(1024)S(1)}) all-reduce(f32[896]{0:T(1024)S(1)} %get-tuple-element.288, f32[896]{0:T(1024)S(1)} %dynamic_update_slice.10, f32[256]{0:T(256)S(1)} %dynamic_update_slice.11, ...), channel_id=3, replica_groups=mesh['seq'=2,'ctx'=8,'wsh'=2] {'seq','ctx','wsh'}, use_global_device_ids=true, to_apply=%region_19.20.clone | all-reduce | flops 2944 | bytes 23552
  664.6 2.0 fusion.33
  666.6 235.9 %reduce-scatter.10.cloned.1.call-done = bf16[56,8320]{1,0:T(8,128)(2,1)} async-done(((bf16[896,8320]{1,0:T(8,128)(2,1)}), bf16[56,8320]{1,0:T(8,128)(2,1)}) %reduce-scatter.10.cloned.1.call-update) | async-done | bytes 931856
  902.5 1.4 convert_element_type.178
  (182 shorter events, 41.9 us)
Async XLA Ops:
  8.0 160.8 %copy-start.1 = (bf16[1,128,896]{2,1,0:T(8,128)(2,1)S(1)}, bf16[1,128,896]{2,1,0:T(8,128)(2,1)}, u32[]{:S(2)}) copy-start(bf16[1,128,896]{2,1,0:T(8,128)(2,1)} %param.19) | copy-start | bytes 688132
  8.0 118.6 %copy-start.17 = (bf16[56,448]{1,0:T(8,128)(2,1)S(1)}, bf16[56,448]{1,0:T(8,128)(2,1)}, u32[]{:S(2)}) copy-start(bf16[56,448]{1,0:T(8,128)(2,1)} %param.23) | copy-start | bytes 150532
  8.0 226.2 %all-reduce.16.cloned.1.call-start = ((), (), s32[]{:S(2)}) async-start(), calls=%async_computation.2 | async-start | bytes 917504 | tf_op jit(solution)/shard_map/psum | solution.py:183
  95.6 31.0 %copy-start.13 = (bf16[896,128]{1,0:T(8,128)(2,1)}, bf16[896,128]{1,0:T(8,128)(2,1)S(1)}, u32[]{:S(2)}) copy-start(bf16[896,128]{1,0:T(8,128)(2,1)S(1)} %all_gather.40) | copy-start | bytes 688132
  171.6 3.0 copy-start.18
  174.5 45.1 %copy-start.2 = (f32[7,128,64]{1,2,0:T(8,128)}, f32[7,128,64]{1,2,0:T(8,128)S(1)}, u32[]{:S(2)}) copy-start(f32[7,128,64]{1,2,0:T(8,128)S(1)} %get-tuple-element.149) | copy-start | bytes 688132
  174.6 45.6 %copy-start.11 = (bf16[7,128,64]{1,2,0:T(8,128)(2,1)}, bf16[7,128,64]{1,2,0:T(8,128)(2,1)S(1)}, u32[]{:S(2)}) copy-start(bf16[7,128,64]{1,2,0:T(8,128)(2,1)S(1)} %convert_element_type.151) | copy-start | bytes 344068
  218.4 77.1 %all-gather.6.cloned.1.call-start = ((), (), s32[]{:S(2)}) async-start(), calls=%async_computation.4 | async-start | bytes 4630528 | tf_op jit(solution)/shard_map/all_gather | solution.py:90
  219.0 154.6 %all-gather.4.cloned.1.call-start = ((), (), s32[]{:S(2)}) async-start(), calls=%async_computation.3 | async-start | bytes 4630528 | tf_op jit(solution)/shard_map/all_gather | solution.py:89
  219.6 232.0 %all-gather.8.cloned.1.call-start = ((), (), s32[]{:S(2)}) async-start(), calls=%async_computation.5 | async-start | bytes 4630528 | tf_op jit(solution)/shard_map/all_gather | solution.py:91
  220.2 262.4 %all-reduce.18.cloned.1.call-start = ((), (), s32[]{:S(2)}) async-start(), calls=%async_computation.6 | async-start | bytes 458752 | tf_op jit(solution)/shard_map/psum | solution.py:216
  456.6 3.4 copy-start.8
  456.6 3.4 copy-start
  465.7 93.2 %reduce-scatter.8.cloned.1.call-start = ((), (), s32[]{:S(2)}) async-start(), calls=%async_computation.7 | async-start | bytes 294912
  465.9 4.6 copy-start.7
  470.6 4.4 copy-start.9
  482.6 3.1 copy-start.12
  484.0 3.1 copy-start.3
  485.3 1.8 copy-start.4
  488.7 1.0 copy-start.15
  489.7 0.7 copy-start.16
  492.0 1.0 copy-start.15
  492.9 0.7 copy-start.16
  495.5 96.6 %all-reduce.20.cloned.1.call-start = ((), (), s32[]{:S(2)}) async-start(), calls=%async_computation.9 | async-start | bytes 917504 | tf_op jit(solution)/shard_map/psum | solution.py:191
  495.5 64.7 %copy-start.14 = (bf16[896,128]{1,0:T(8,128)(2,1)S(1)}, bf16[896,128]{1,0:T(8,128)(2,1)}, u32[]{:S(2)}) copy-start(bf16[896,128]{1,0:T(8,128)(2,1)} %copy-done.13) | copy-start | bytes 688132
  562.4 340.1 %reduce-scatter.10.cloned.1.call-start = ((), (), s32[]{:S(2)}) async-start(), calls=%async_computation.8 | async-start | bytes 15841280
  591.4 1.0 copy-start.10
  591.4 73.2 %copy-start.5 = (f32[128,896]{1,0:T(8,128)S(1)}, f32[128,896]{1,0:T(8,128)}, u32[]{:S(2)}) copy-start(f32[128,896]{1,0:T(8,128)} %copy-done.4) | copy-start | bytes 1376260
  902.5 2.1 copy-start.6
Sparse Core Ops, SparseCore 0:
  218.5 15.6 all-reduce.15
  465.8 16.7 all-reduce.17
  495.6 63.3 reduce-scatter.7
  562.5 17.6 all-reduce.19
Sparse Core Ops, SparseCore 1:
  221.7 73.8 all-gather.5
  298.2 75.3 all-gather.3
  376.3 75.3 all-gather.7
  591.5 310.9 reduce-scatter.9
where the time goes:
time: 916 us; the launch traced here: 915 us
  waiting for transfers between devices  524 us (57%)
  blocking collectives  263 us (29%)
  matrix products  52 us (6%)
  local copies, waits for them, and re-layouts  44.2 us (5%)
  between operations  16 us (2%)
  other arithmetic  14.3 us (2%)
    unnamed x10, waiting for transfers between devices  298 us
    unnamed x2, blocking collectives  111 us
    all_gather x1, waiting for transfers between devices, per_device(): lax.all_gather(w_down, ('seq', 'ctx'), axis=1, tiled=True)  73.9 us
    all_gather x1, waiting for transfers between devices, per_device(): lax.all_gather(w_gate, ('seq', 'ctx'), axis=0, tiled=True)  73.9 us
    all_gather x1, waiting for transfers between devices, per_device(): lax.all_gather(w_up, ('seq', 'ctx'), axis=0, tiled=True)  60.1 us
    all_gather x1, blocking collectives, per_device(): lax.all_gather(w_output, ('seq', 'ctx'), axis=1, tiled=True)  42.6 us
    all_gather x1, blocking collectives, per_device(): lax.all_gather(w_query, ('seq', 'ctx'), axis=0, tiled=True)  42.1 us
    all_gather x1, blocking collectives, per_device(): lax.all_gather(w_keyvalue, ('seq', 'ctx'), axis=0, tiled=True)  41 us
  transfers between devices with their start and end apart: 8, of which 7 were waited for; matrix products, arithmetic and copies ran while one was open for 7% of the time, Pallas kernels for 0%

commit v1 on v0

--- a/solution.py
+++ b/solution.py
@@ -7,6 +7,18 @@
 HD = 64
 epsilon = 1e-06
 theta_log = math.log(1000000.0)
+
+
+def collect(array, axis, dim):
+    ways, here, step = (lax.axis_size(axis), lax.axis_index(axis), array.shape[dim])
+    line, have = (array, 1)
+    while have < ways:
+        line = jnp.concatenate(
+            [line, lax.ppermute(line, axis, [(d, (d - have) % ways) for d in range(ways)])],
+            axis=dim,
+        )
+        have = 2 * have
+    return jnp.roll(line, here * step, axis=dim)
 
 
 def partner(block, axis, stride):
@@ -88,7 +100,7 @@
         lax.all_gather(w_output, ("seq", "ctx"), axis=1, tiled=True),
         lax.all_gather(w_gate, ("seq", "ctx"), axis=0, tiled=True),
         lax.all_gather(w_up, ("seq", "ctx"), axis=0, tiled=True),
-        lax.all_gather(w_down, ("seq", "ctx"), axis=1, tiled=True),
+        collect(w_down, ("seq", "ctx"), 1),
     )
     g_one, bias_q, bias_kv, g_two = (
         lax.all_gather(attn_gain, ("seq", "ctx", "wsh"), axis=0, tiled=True),

time: 916 us -> 960 us (1.048)
  waiting for transfers between devices: 524 us -> 547 us
  local copies, waits for them, and re-layouts: 44.2 us -> 61.8 us
    ppermute x0 -> x4, waiting for transfers between devices: none -> 103 us  [collect(): lax.ppermute(line, axis, [(d, (d - have) % ways) for d in range(ways)])]
    all_gather x1, waiting for transfers between devices: 73.9 us -> 0.01 us  [per_device(): lax.all_gather(w_gate, ('seq', 'ctx'), axis=0, tiled=True)]
    psum x1, waiting for transfers between devices: 13.9 us -> 0.01 us  [per_device(): lax.psum(jnp.dot(attended_low, wo_full, preferred_element_type=jnp.float3...]
    unnamed x50 -> x101, local copies, waits for them, and re-layouts: 8.59 us -> 18.3 us
  transfers between devices with their start and end apart: 8 -> 12, of which waited for: 7 -> 9; matrix products, arithmetic and copies ran while one was open for 7% -> 8% of each run, Pallas kernels for 0% -> 0%
where the time goes in v1:
time: 960 us; the launch traced here: 958 us
  waiting for transfers between devices  547 us (57%)
  blocking collectives  262 us (27%)
  local copies, waits for them, and re-layouts  61.8 us (6%)
  matrix products  50 us (5%)
  other arithmetic  16.7 us (2%)
  between operations  16.2 us (2%)
    unnamed x10, waiting for transfers between devices  298 us
    unnamed x2, blocking collectives  108 us
    ppermute x4, waiting for transfers between devices, collect(): lax.ppermute(line, axis, [(d, (d - have) % ways) for d in range(ways)])  103 us
    all_gather x1, waiting for transfers between devices, per_device(): lax.all_gather(w_down, ('seq', 'ctx'), axis=1, tiled=True)  73.9 us
    all_gather x1, waiting for transfers between devices, per_device(): lax.all_gather(w_up, ('seq', 'ctx'), axis=0, tiled=True)  63.1 us
    all_gather x1, blocking collectives, per_device(): lax.all_gather(w_output, ('seq', 'ctx'), axis=1, tiled=True)  44.1 us
    all_gather x1, blocking collectives, per_device(): lax.all_gather(w_query, ('seq', 'ctx'), axis=0, tiled=True)  41.7 us
    all_gather x1, blocking collectives, per_device(): lax.all_gather(w_keyvalue, ('seq', 'ctx'), axis=0, tiled=True)  41.2 us
  transfers between devices with their start and end apart: 12, of which 9 were waited for; matrix products, arithmetic and copies ran while one was open for 8% of the time, Pallas kernels for 0%

profile of v1, /device:TPU:0, one launch (start us, length us, event | category | flops | bytes accessed | tf_op | source)
XLA Modules:
  0.0 957.9 jit_solution(2432339278425962991)
XLA Ops:
  11.5 42.1 %all-reduce.10 = (bf16[256]{0:T(256)(128)(2,1)S(1)}, bf16[896]{0:T(1024)(128)(2,1)S(1)}, bf16[896]{0:T(1024)(128)(2,1)S(1)}, bf16[896]{0:T(1024)(128)(2,1)}) all-reduce(bf16[256]{0:T(256)(128)(2,1)S(1)} %dynamic-update-slice.1, bf16[896]{0:T(1024)(128)(2,1)S(1)} %dynamic-update-slice, ...), channel_id=1, replica_groups=mesh['seq'=2,'ctx'=8,'wsh'=2] {'seq','ctx','wsh'}, use_global_device_ids=true, to_apply=%add.1 | all-reduce | flops 2944 | bytes 11776
  54.7 41.2 %all_gather.39 = bf16[896,128]{1,0:T(8,128)(2,1)S(1)} all-gather(bf16[56,128]{1,0:T(8,128)(2,1)} %param.25), channel_id=1, replica_groups=mesh['seq'=2,'ctx'=8,'wsh'=2] {'seq','ctx'}, dimensions={0}, use_global_device_ids=true | all-gather | bytes 243712 | tf_op jit(solution)/shard_map/all_gather | solution.py:99
  98.9 26.7 %all_gather.41 = bf16[1024,128]{0,1:T(8,128)(2,1)S(1)} all-gather(bf16[128,128]{0,1:T(8,128)(2,1)S(1)} %pad_maximum_fusion.4), channel_id=1, replica_groups=mesh['seq'=2,'ctx'=8,'wsh'=2] {'ctx'}, dimensions={0}, use_global_device_ids=true | all-gather | bytes 294912 | tf_op jit(solution)/shard_map/all_gather | solution.py:139
  125.6 41.7 %all_gather.42 = bf16[896,448]{1,0:T(8,128)(2,1)S(1)} all-gather(bf16[56,448]{1,0:T(8,128)(2,1)S(1)} %copy-done.24), channel_id=1, replica_groups=mesh['seq'=2,'ctx'=8,'wsh'=2] {'seq','ctx'}, dimensions={0}, use_global_device_ids=true | all-gather | bytes 852992 | tf_op jit(solution)/shard_map/all_gather | solution.py:98
  169.9 3.5 while.39
  173.5 6.6 while.40
  180.1 44.1 %all_gather.44 = bf16[448,896]{0,1:T(8,128)(2,1)S(1)} all-gather(bf16[448,56]{0,1:T(8,128)(2,1)S(1)} %copy-done.25), channel_id=1, replica_groups=mesh['seq'=2,'ctx'=8,'wsh'=2] {'seq','ctx'}, dimensions={1}, use_global_device_ids=true | all-gather | bytes 852992 | tf_op jit(solution)/shard_map/all_gather | solution.py:100
  228.7 5.5 collective-permute-done
  234.9 21.3 %collective-permute-done.1 = bf16[2432,112]{0,1:T(8,128)(2,1)S(1)} collective-permute-done((bf16[2432,112]{0,1:T(8,128)(2,1)S(1)}, bf16[2432,112]{0,1:T(8,128)(2,1)S(1)}, u32[]{:S(2)}, u32[]{:S(2)}) %collective-permute-start.1) | collective-permute-done | bytes 544800 | tf_op jit(solution)/shard_map/ppermute | solution.py:17
  256.8 39.2 %collective-permute-done.2 = bf16[2432,224]{0,1:T(8,128)(2,1)S(1)} collective-permute-done((bf16[2432,224]{0,1:T(8,128)(2,1)S(1)}, bf16[2432,224]{0,1:T(8,128)(2,1)S(1)}, u32[]{:S(2)}, u32[]{:S(2)}) %collective-permute-start.2) | collective-permute-done | bytes 1089568 | tf_op jit(solution)/shard_map/ppermute | solution.py:17
  303.7 36.7 %collective-permute-done.3 = bf16[2432,448]{0,1:T(8,128)(2,1)} collective-permute-done((bf16[2432,448]{0,1:T(8,128)(2,1)}, bf16[2432,448]{0,1:T(8,128)(2,1)}, u32[]{:S(2)}, u32[]{:S(2)}) %collective-permute-start.3) | collective-permute-done | bytes 2179104 | tf_op jit(solution)/shard_map/ppermute | solution.py:17
  340.4 3.1 constant_dynamic-update-slice_fusion.5
  347.0 3.2 constant_dynamic-update-slice_fusion
  350.2 4.2 fusion.81
  354.4 63.1 %all-gather.6.cloned.1.call-done = bf16[896,2432]{1,0:T(8,128)(2,1)} async-done(((bf16[56,2432]{1,0:T(8,128)(2,1)}), bf16[896,2432]{1,0:T(8,128)(2,1)}) %all-gather.6.cloned.1.call-update) | async-done | bytes 4358160 | tf_op jit(solution)/shard_map/all_gather | solution.py:102
  417.4 4.1 fusion.82
  421.6 73.9 %all-gather.8.cloned.1.call-done = bf16[2432,896]{0,1:T(8,128)(2,1)} async-done(((bf16[2432,56]{0,1:T(8,128)(2,1)}), bf16[2432,896]{0,1:T(8,128)(2,1)}) %all-gather.8.cloned.1.call-update) | async-done | bytes 4358160 | tf_op jit(solution)/shard_map/all_gather | solution.py:213
  495.5 4.1 multiply_convert_fusion
  499.6 3.6 convolution_convert_fusion.1
  503.1 3.4 convolution_convert_fusion.2
  507.9 2.2 fusion.78
  510.3 3.4 fusion.14
  513.8 4.3 fusion.18
  518.1 8.8 all-reduce.18.cloned.1.call-done
  531.0 6.1 while.41
  539.6 2.2 copy.48
  543.1 58.4 %reduce-scatter.8.cloned.1.call-done = bf16[128,128]{1,0:T(8,128)(2,1)} async-done(((bf16[1024,128]{1,0:T(8,128)(2,1)}), bf16[128,128]{1,0:T(8,128)(2,1)}) %reduce-scatter.8.cloned.1.call-update) | async-done | bytes 32784
  606.0 2.3 copy.50
  608.8 26.1 %concatenate.57 = bf16[896,8320]{1,0:T(8,128)(2,1)} concatenate(bf16[896,448]{1,0:T(8,128)(2,1)S(1)} %copy-done.10, bf16[896,128]{1,0:T(8,128)(2,1)S(1)} %copy.49, bf16[896,448]{1,0:T(8,128)(2,1)} %copy.50, bf16[896,2432]{1,0:T(8,128)(2,1)} %convolution_convert_fusion.2, bf16[896,2432]{1,0:T(8,128)(2,1)} %convolution_convert_fusion.1, bf16[896,2432]{1,0:T(8,128)(2,1)} %fusion.14), dimensions={1} | concatenate | bytes 29818880 | tf_op jit(solution)/shard_map/concatenate | solution.py:302
  636.7 65.9 %all-reduce.9 = (f32[896]{0:T(1024)S(1)}, f32[896]{0:T(1024)S(1)}, f32[256]{0:T(256)S(1)}, f32[896]{0:T(1024)S(1)}) all-reduce(f32[896]{0:T(1024)S(1)} %get-tuple-element.288, f32[896]{0:T(1024)S(1)} %dynamic_update_slice.10, f32[256]{0:T(256)S(1)} %dynamic_update_slice.11, ...), channel_id=3, replica_groups=mesh['seq'=2,'ctx'=8,'wsh'=2] {'seq','ctx','wsh'}, use_global_device_ids=true, to_apply=%region_19.20.clone | all-reduce | flops 2944 | bytes 23552
  705.0 2.0 fusion.38
  707.0 238.8 %reduce-scatter.10.cloned.1.call-done = bf16[56,8320]{1,0:T(8,128)(2,1)} async-done(((bf16[896,8320]{1,0:T(8,128)(2,1)}), bf16[56,8320]{1,0:T(8,128)(2,1)}) %reduce-scatter.10.cloned.1.call-update) | async-done | bytes 931856
  (239 shorter events, 65.7 us)
Async XLA Ops:
  8.0 161.2 %copy-start = (bf16[1,128,896]{2,1,0:T(8,128)(2,1)S(1)}, bf16[1,128,896]{2,1,0:T(8,128)(2,1)}, u32[]{:S(2)}) copy-start(bf16[1,128,896]{2,1,0:T(8,128)(2,1)} %param.19) | copy-start | bytes 688132
  8.0 159.9 %copy-start.30 = (s32[1,1024]{1,0:T(1,128)S(1)}, s32[1,1024]{1,0:T(1,128)}, u32[]{:S(2)}) copy-start(s32[1,1024]{1,0:T(1,128)} %param.21) | copy-start | bytes 12292
  8.0 117.6 %copy-start.24 = (bf16[56,448]{1,0:T(8,128)(2,1)S(1)}, bf16[56,448]{1,0:T(8,128)(2,1)}, u32[]{:S(2)}) copy-start(bf16[56,448]{1,0:T(8,128)(2,1)} %param.23) | copy-start | bytes 150532
  8.0 292.4 %all-reduce.16.cloned.1.call-start = ((), (), s32[]{:S(2)}) async-start(), calls=%async_computation.2 | async-start | bytes 917504 | tf_op jit(solution)/shard_map/psum | solution.py:195
  8.1 161.7 %copy-start.31 = (f32[32]{0:T(128)}, f32[32]{0:T(128)S(1)}, u32[]{:S(2)}) copy-start(f32[32]{0:T(128)S(1)} %multiply_exponential_fusion) | copy-start | bytes 388
  53.6 116.2 %copy-start.17 = (f32[896]{0:T(1024)}, f32[896]{0:T(1024)S(1)}, u32[]{:S(2)}) copy-start(f32[896]{0:T(1024)S(1)} %convert_element_type.145) | copy-start | bytes 10756
  54.7 115.1 %copy-start.26 = (f32[128]{0:T(128)}, f32[128]{0:T(128)S(1)}, u32[]{:S(2)}) copy-start(f32[128]{0:T(128)S(1)} %add_rsqrt_fusion.1) | copy-start | bytes 1540
  97.9 71.9 %copy-start.28 = (f32[128]{0:T(128)}, f32[128]{0:T(128)S(1)}, u32[]{:S(2)}) copy-start(f32[128]{0:T(128)S(1)} %get-tuple-element.354) | copy-start | bytes 1540
  98.7 71.2 %copy-start.19 = (f32[128,32]{0,1:T(8,128)}, f32[128,32]{0,1:T(8,128)S(1)}, u32[]{:S(2)}) copy-start(f32[128,32]{0,1:T(8,128)S(1)} %get-tuple-element.375) | copy-start | bytes 49156
  180.0 54.1 %copy-start.21 = (s32[128]{0:T(128)}, s32[128]{0:T(128)S(1)}, u32[]{:S(2)}) copy-start(s32[128]{0:T(128)S(1)} %get-tuple-element.680) | copy-start | bytes 1540
  180.0 47.6 %copy-start.1 = (bf16[2432,56]{0,1:T(8,128)(2,1)S(1)}, bf16[2432,56]{0,1:T(8,128)(2,1)}, u32[]{:S(2)}) copy-start(bf16[2432,56]{0,1:T(8,128)(2,1)} %param.31) | copy-start | bytes 817156
  180.1 54.1 %copy-start.2 = (bf16[2432,56]{0,1:T(8,128)(2,1)S(1)}, bf16[2432,56]{0,1:T(8,128)(2,1)}, u32[]{:S(2)}) copy-start(bf16[2432,56]{0,1:T(8,128)(2,1)} %param.31) | copy-start | bytes 817156
  180.1 44.1 %copy-start.11 = (bf16[7,128,64]{1,2,0:T(8,128)(2,1)}, bf16[7,128,64]{1,2,0:T(8,128)(2,1)S(1)}, u32[]{:S(2)}) copy-start(bf16[7,128,64]{1,2,0:T(8,128)(2,1)S(1)} %convert_element_type.151) | copy-start | bytes 344068
  226.4 123.8 %all-gather.4.cloned.1.call-start = ((), (), s32[]{:S(2)}) async-start(), calls=%async_computation.3 | async-start | bytes 4630528 | tf_op jit(solution)/shard_map/all_gather | solution.py:101
  227.0 190.4 %all-gather.6.cloned.1.call-start = ((), (), s32[]{:S(2)}) async-start(), calls=%async_computation.4 | async-start | bytes 4630528 | tf_op jit(solution)/shard_map/all_gather | solution.py:102
  227.6 267.9 %all-gather.8.cloned.1.call-start = ((), (), s32[]{:S(2)}) async-start(), calls=%async_computation.5 | async-start | bytes 4630528 | tf_op jit(solution)/shard_map/all_gather | solution.py:213
  227.6 6.5 collective-permute-start
  228.6 298.4 %all-reduce.18.cloned.1.call-start = ((), (), s32[]{:S(2)}) async-start(), calls=%async_computation.6 | async-start | bytes 458752 | tf_op jit(solution)/shard_map/psum | solution.py:228
  234.2 65.5 %copy-start.7 = (bf16[2432,56]{0,1:T(8,128)(2,1)}, bf16[2432,56]{0,1:T(8,128)(2,1)S(1)}, u32[]{:S(2)}) copy-start(bf16[2432,56]{0,1:T(8,128)(2,1)S(1)} %collective-permute-done) | copy-start | bytes 817156
  234.2 21.9 %collective-permute-start.1 = (bf16[2432,112]{0,1:T(8,128)(2,1)S(1)}, bf16[2432,112]{0,1:T(8,128)(2,1)S(1)}, u32[]{:S(2)}, u32[]{:S(2)}) collective-permute-start(bf16[2432,112]{0,1:T(8,128)(2,1)S(1)} %pad_maximum_fusion.2), channel_id=1, source_target_pairs={{0,28},{2,30},{4,0},{6,2},{8,4},{10,6},{12,8},{14,10},{16,12},{18,... | collective-permute-start | bytes 1634312 | tf_op jit(solution)/shard_map/ppermute | solution.py:17
  256.2 42.7 %copy-start.33 = (bf16[896]{0:T(1024)(128)(2,1)S(1)}, bf16[896]{0:T(1024)(128)(2,1)}, u32[]{:S(2)}) copy-start(bf16[896]{0:T(1024)(128)(2,1)} %get-tuple-element.347) | copy-start | bytes 5380
  256.2 39.8 %collective-permute-start.2 = (bf16[2432,224]{0,1:T(8,128)(2,1)S(1)}, bf16[2432,224]{0,1:T(8,128)(2,1)S(1)}, u32[]{:S(2)}, u32[]{:S(2)}) collective-permute-start(bf16[2432,224]{0,1:T(8,128)(2,1)S(1)} %pad_maximum_fusion.1), channel_id=1, source_target_pairs={{0,24},{2,26},{4,28},{6,30},{8,0},{10,2},{12,4},{14,6},{16,8},{18,... | collective-permute-start | bytes 3268616 | tf_op jit(solution)/shard_map/ppermute | solution.py:17
  297.6 42.9 %collective-permute-start.3 = (bf16[2432,448]{0,1:T(8,128)(2,1)}, bf16[2432,448]{0,1:T(8,128)(2,1)}, u32[]{:S(2)}, u32[]{:S(2)}) collective-permute-start(bf16[2432,448]{0,1:T(8,128)(2,1)} %pad_maximum_fusion), channel_id=1, source_target_pairs={{0,16},{2,18},{4,20},{6,22},{8,24},{10,26},{12,28},{14,30},{16,0},... | collective-permute-start | bytes 6537224 | tf_op jit(solution)/shard_map/ppermute | solution.py:17
  303.7 40.6 %copy-start.8 = (bf16[2432,56]{0,1:T(8,128)(2,1)S(1)}, bf16[2432,56]{0,1:T(8,128)(2,1)}, u32[]{:S(2)}) copy-start(bf16[2432,56]{0,1:T(8,128)(2,1)} %copy-done.7) | copy-start | bytes 817156
  354.4 141.1 %copy-start.13 = (bf16[1,128,896]{2,1,0:T(8,128)(2,1)S(1)}, bf16[1,128,896]{2,1,0:T(8,128)(2,1)}, u32[]{:S(2)}) copy-start(bf16[1,128,896]{2,1,0:T(8,128)(2,1)} %param.20) | copy-start | bytes 688132
  510.1 91.4 %reduce-scatter.8.cloned.1.call-start = ((), (), s32[]{:S(2)}) async-start(), calls=%async_computation.7 | async-start | bytes 294912
  538.0 97.6 %all-reduce.20.cloned.1.call-start = ((), (), s32[]{:S(2)}) async-start(), calls=%async_computation.9 | async-start | bytes 917504 | tf_op jit(solution)/shard_map/psum | solution.py:203
  538.3 64.2 %copy-start.29 = (f32[128]{0:T(128)S(1)}, f32[128]{0:T(128)}, u32[]{:S(2)}) copy-start(f32[128]{0:T(128)} %copy-done.28) | copy-start | bytes 1540
  538.3 64.2 %copy-start.32 = (f32[32]{0:T(128)S(1)}, f32[32]{0:T(128)}, u32[]{:S(2)}) copy-start(f32[32]{0:T(128)} %copy-done.31) | copy-start | bytes 388
  538.3 64.4 %copy-start.15 = (bf16[896,128]{1,0:T(8,128)(2,1)S(1)}, bf16[896,128]{1,0:T(8,128)(2,1)}, u32[]{:S(2)}) copy-start(bf16[896,128]{1,0:T(8,128)(2,1)} %copy-done.14) | copy-start | bytes 688132
  541.9 62.9 %copy-start.12 = (bf16[7,128,64]{1,2,0:T(8,128)(2,1)S(1)}, bf16[7,128,64]{1,2,0:T(8,128)(2,1)}, u32[]{:S(2)}) copy-start(bf16[7,128,64]{1,2,0:T(8,128)(2,1)} %copy-done.11) | copy-start | bytes 344068
  604.7 341.1 %reduce-scatter.10.cloned.1.call-start = ((), (), s32[]{:S(2)}) async-start(), calls=%async_computation.8 | async-start | bytes 15841280
  (18 other events, 121.5 us)
Sparse Core Ops, SparseCore 0:
  226.5 15.8 all-reduce.15
  510.2 16.7 all-reduce.17
  538.1 63.2 reduce-scatter.7
  604.8 17.6 all-reduce.19
Sparse Core Ops, SparseCore 1:
  229.7 108.7 all-gather.3
  341.1 76.2 all-gather.5
  420.1 75.3 all-gather.7
  635.0 310.8 reduce-scatter.9
